TPU v7x, 32 devices: a whole 2x2x4 slice. The times are simulated.
32 devices in a mesh: blk: 8 (over z, core), tp: 4 (over y, x).
Axes of the slice: x: 2, y: 2, z: 4, core: 2. Of those that a mesh axis runs over, the one named last changes fastest.
Arguments:
- tokens: bfloat16 [2048, 5120], P('blk', 'tp'), may hold values from -31 to 31
- norm_gain: bfloat16 [5120], P('tp'), may hold values from 0.15 to 2
- w_query: bfloat16 [5120, 5120], P(None, 'tp'), may hold values from -0.078125 to 0.078125
- w_key: bfloat16 [5120, 1024], P(None, 'tp'), may hold values from -0.078125 to 0.078125
- w_value: bfloat16 [5120, 1024], P(None, 'tp'), may hold values from -0.078125 to 0.078125
- query_bias: bfloat16 [5120], P('tp'), may hold values from -45 to 45
- key_bias: bfloat16 [1024], P('tp'), may hold values from -45 to 45
- value_bias: bfloat16 [1024], P('tp'), may hold values from -4 to 4
- lengths: int32 [8], replicated, may hold values from 1 to 1024, 2048 in all
- page_table: int32 [16], replicated, may hold values from 0 to 15, as said below
Outputs:
- attended: bfloat16 [2048, 5120], P('blk', 'tp')
- kv_cache: bfloat16 [16, 2, 128, 1024], P('blk', None, None, 'tp')
Inputs may be any that keep to these rules, and one draw needn't show every extreme that they name: `lengths`: the last piece is padding; the others are prompts. `page_table`: A permutation of the 16 slots; slot s belongs to index s // 2 of blk.
All inputs are finite; a program needn't handle non-finite values.
Results may differ from a plain program's by a relative error of at most 0.012.
The roundings to bfloat16 on the way count: a program that leaves them out, or rounds other values in their place, can miss the bound.
Values may be sent and summed in bfloat16 or wider, within the bound.
No kernel may reach another device: no remote copies, remote signals or barrier semaphores. Data moves between devices by JAX's collectives and lax.ppermute only.
A program may use at most 128 MiB of HBM per device.

v0:
```python
import jax
import jax.numpy as jnp
from jax import lax
from jax.sharding import PartitionSpec as P

D = 5120
HEADS = 40
KV_HEADS = 8
HEAD = 128
PAGE = 128


rope_base = 1000000.0
norm_eps = 1e-06
neg_large = -1e30


def token_meta(positions, lengths):
    ends = jnp.cumsum(lengths)
    past = (positions[:, None] >= ends[None, :]).astype(jnp.int32)
    segment = jnp.sum(past, axis=1)
    start = jnp.sum(past * lengths[None, :], axis=1)
    return (segment, positions - start)


def rotate(values, offsets):
    half = HEAD // 2
    freq = rope_base ** (-2.0 * jnp.arange(half, dtype=jnp.float32) / HEAD)
    angle = offsets.astype(jnp.float32)[:, None] * freq[None, :]
    cosine = jnp.cos(angle)[:, None, :]
    sine = jnp.sin(angle)[:, None, :]
    first = values[..., :half]
    second = values[..., half:]
    return jnp.concatenate(
        [first * cosine - second * sine, second * cosine + first * sine], axis=-1
    )


def on_device(
    tokens,
    norm_gain,
    w_query,
    w_key,
    w_value,
    query_bias,
    key_bias,
    value_bias,
    lengths,
    page_table,
):
    rows = tokens.shape[0]
    blocks = lax.axis_size("blk")
    me = lax.axis_index("blk")
    q_width = w_query.shape[1]
    kv_width = w_key.shape[1]
    kv_dev = kv_width // HEAD
    group = HEADS // KV_HEADS
    slots = rows // PAGE
    docs = lengths.shape[0]
    scale = 1.0 / float(HEAD) ** 0.5
    wide = tokens.astype(jnp.float32)
    scaled = (wide * norm_gain.astype(jnp.float32)).astype(jnp.bfloat16)
    empty = (
        jnp.zeros((rows, q_width), jnp.float32),
        jnp.zeros((rows, kv_width), jnp.float32),
        jnp.zeros((rows, kv_width), jnp.float32),
    )
    piece = lax.all_gather(scaled, "tp", axis=1, tiled=True)
    count = piece.shape[1]
    totals = []
    for total, weight in zip(empty, (w_query, w_key, w_value)):
        totals.append(jnp.dot(piece, weight, preferred_element_type=jnp.float32))
    proj_query, proj_key, proj_value = tuple(totals)
    squares = lax.psum(jnp.sum(wide * wide, axis=1), "tp")
    rstd = lax.rsqrt(squares / D + norm_eps)
    own_pos = me * rows + jnp.arange(rows, dtype=jnp.int32)
    own_seg, own_off = token_meta(own_pos, lengths)
    own_live = own_seg < docs - 1
    query = rstd[:, None] * proj_query + query_bias.astype(jnp.float32)
    key = rstd[:, None] * proj_key + key_bias.astype(jnp.float32)
    value = rstd[:, None] * proj_value + value_bias.astype(jnp.float32)
    query = (
        rotate(query.reshape(rows, q_width // HEAD, HEAD), own_off)
        .reshape(rows, q_width)
        .astype(jnp.bfloat16)
    )
    key = (
        jnp.where(own_live[:, None, None], rotate(key.reshape(rows, kv_dev, HEAD), own_off), 0.0)
        .reshape(rows, kv_width)
        .astype(jnp.bfloat16)
    )
    value = jnp.where(own_live[:, None], value, 0.0).astype(jnp.bfloat16)
    q_seg, q_off = token_meta(own_pos, lengths)
    q_live = q_seg < docs - 1
    q_lo = jnp.min(jnp.where(q_live, own_pos - q_off, blocks * rows))
    q_hi = jnp.max(own_pos)
    q_grouped = query.reshape(rows, kv_dev, group, HEAD)

    def attend(state, key_block, value_block, key_start):
        best, total, acc = state
        count = key_block.shape[0]
        k_pos = key_start + jnp.arange(count, dtype=jnp.int32)
        k_seg, k_off = token_meta(k_pos, lengths)
        allowed = (
            (k_seg[None, :] == q_seg[:, None])
            & (k_pos[None, :] <= own_pos[:, None])
            & q_live[:, None]
        )
        scores = (
            jnp.einsum(
                "qcgh,tch->cgqt",
                q_grouped,
                key_block.reshape(count, kv_dev, HEAD),
                preferred_element_type=jnp.float32,
            )
            * scale
        )
        scores = jnp.where(allowed, scores, neg_large)
        fresh = jnp.maximum(best, jnp.max(scores, axis=3))
        expo = jnp.where(allowed, jnp.exp(scores - fresh[..., None]), 0.0)
        shrink = jnp.exp(best - fresh)
        total = total * shrink + jnp.sum(expo, axis=3)
        acc = acc * shrink[..., None] + jnp.einsum(
            "cgqt,tch->cgqh",
            expo.astype(jnp.bfloat16),
            value_block.reshape(count, kv_dev, HEAD),
            preferred_element_type=jnp.float32,
        )
        return (fresh, total, acc)

    start_state = (
        jnp.full((kv_dev, group, rows), neg_large, jnp.float32),
        jnp.zeros((kv_dev, group, rows), jnp.float32),
        jnp.zeros((kv_dev, group, rows, HEAD), jnp.float32),
    )
    start_state = start_state + (
        jnp.zeros((slots, PAGE * kv_width), jnp.float32),
        jnp.zeros((slots, PAGE * kv_width), jnp.float32),
    )
    key_piece = lax.all_gather(key, "blk", axis=0, tiled=True)
    value_piece = lax.all_gather(value, "blk", axis=0, tiled=True)
    count = key_piece.shape[0]
    step = 512

    def one_step(index, state):
        first = index * step
        key_block = lax.dynamic_slice_in_dim(key_piece, first, step, 0)
        value_block = lax.dynamic_slice_in_dim(value_piece, first, step, 0)
        needed = (first <= q_hi) & (first + step - 1 >= q_lo)
        return lax.cond(
            needed,
            lambda held: attend(held, key_block, value_block, first),
            lambda held: held,
            state,
        )

    attention = lax.fori_loop(
        0, count // step, one_step, (start_state[0], start_state[1], start_state[2])
    )
    pages_here = count // PAGE
    pick = (page_table[None, :] == me * slots + jnp.arange(slots, dtype=jnp.int32)[:, None]).astype(
        jnp.bfloat16
    )
    cache_keys = jnp.dot(
        pick, key_piece.reshape(pages_here, PAGE * kv_width), preferred_element_type=jnp.float32
    )
    cache_values = jnp.dot(
        pick, value_piece.reshape(pages_here, PAGE * kv_width), preferred_element_type=jnp.float32
    )
    folded = attention + (cache_keys, cache_values)
    mixed = folded[2] / jnp.where(q_live, folded[1], 1.0)[..., None]
    mixed = jnp.transpose(mixed, (2, 0, 1, 3)).reshape(rows, q_width)
    mixed = jnp.where(q_live[:, None], mixed, 0.0).astype(jnp.bfloat16)
    kv_cache = (
        jnp.stack([folded[3], folded[4]], axis=1)
        .reshape(slots, 2, PAGE, kv_width)
        .astype(jnp.bfloat16)
    )
    return (mixed, kv_cache)


def solution(mesh):
    in_specs = (
        P("blk", "tp"),
        P("tp"),
        P(None, "tp"),
        P(None, "tp"),
        P(None, "tp"),
        P("tp"),
        P("tp"),
        P("tp"),
        P(),
        P(),
    )
    out_specs = (P("blk", "tp"), P("blk", None, None, "tp"))
    return jax.shard_map(
        on_device, mesh=mesh, in_specs=in_specs, out_specs=out_specs, check_vma=False
    )
```

profile of v0, /device:TPU:24, one launch (start us, length us, event | category | flops | bytes accessed | tf_op | source)
XLA Modules:
  0.0 155.5 jit_solution(7816124166424336681)
XLA Ops:
  8.1 2.1 %fusion.15 = (f32[256]{0:T(256)S(1)}, bf16[256,1280]{1,0:T(8,128)(2,1)}) fusion(bf16[256,1280]{1,0:T(8,128)(2,1)} %param.14, f32[1280]{0:T(1024)S(1)} %convert_element_type.73), kind=kLoop, calls=%fused_computation.24 | loop fusion | flops 1638144 | bytes 1316864 | tf_op jit(solution)/shard_map/reduce_sum | solution.py:74
  11.7 9.9 %psum.7 = f32[256]{0:T(256)S(1)} all-reduce(f32[256]{0:T(256)S(1)} %get-tuple-element.683), channel_id=1, replica_groups=mesh['blk'=8,'tp'=4] {'tp'}, use_global_device_ids=true, to_apply=%region_3.4 | all-reduce | flops 256 | bytes 2048 | tf_op jit(solution)/shard_map/psum | solution.py:74
  23.4 27.7 %all-gather.4.cloned.1.call-done = bf16[256,5120]{1,0:T(8,128)(2,1)} async-done(((bf16[256,1280]{1,0:T(8,128)(2,1)}), bf16[256,5120]{1,0:T(8,128)(2,1)}) %all-gather.4.cloned.1.call-update) | async-done | bytes 2621456 | tf_op jit(solution)/shard_map/all_gather | solution.py:68
  51.1 2.9 %fusion.18 = f32[256,256]{0,1:T(8,128)S(1)} fusion(bf16[256,5120]{1,0:T(8,128)(2,1)} %all-gather.4.cloned.1.call-done, bf16[5120,256]{1,0:T(8,128)(2,1)S(1)} %copy-done, f32[256]{0:T(256)S(1)} %convert_element_type.75, f32[256]{0:T(256)S(1)} %add_rsqrt_fusion), kind=kOutput, calls=%fused_computation.30 | convolution fusion | flops 671219712 | bytes 5507072 | tf_op jit(solution)/shard_map/dot_general | solution.py:72
  54.9 4.4 %fusion.21 = bf16[256,256]{0,1:T(8,128)(2,1)} fusion(bf16[256,5120]{1,0:T(8,128)(2,1)} %all-gather.4.cloned.1.call-done, bf16[5120,256]{1,0:T(8,128)(2,1)} %param.18, f32[256]{0:T(256)S(1)} %convert_element_type.80, f32[256]{0:T(256)S(1)} %add_rsqrt_fusion, pred[256]{0:T(512)(128)(4,1)S(1)} %get-tuple-element.789), kind=kOutput, calls=%fused_computation.33 | convolution fusion | flops 671350784 | bytes 5376256 | tf_op jit(solution)/shard_map/dot_general | solution.py:72
  59.9 10.3 %fusion.14 = f32[256,1280]{1,0:T(8,128)} fusion(bf16[256,5120]{1,0:T(8,128)(2,1)} %all-gather.4.cloned.1.call-done, bf16[5120,1280]{1,0:T(8,128)(2,1)} %param.16, f32[1280]{0:T(1024)S(1)} %convert_element_type.78, f32[256]{0:T(256)S(1)} %add_rsqrt_fusion), kind=kOutput, calls=%fused_computation.21 | convolution fusion | flops 3356098560 | bytes 17045504 | tf_op jit(solution)/shard_map/dot_general | solution.py:72
  70.2 2.8 %copy.37 = f32[256,1280]{0,1:T(8,128)} copy(f32[256,1280]{1,0:T(8,128)} %fusion.14) | data formatting | bytes 2621440 | tf_op jit(solution)/shard_map/add | solution.py:79
  73.0 1.5 subtract_convert_fusion
  77.8 24.2 %all-gather.8.cloned.1.call-done = bf16[2048,256]{0,1:T(8,128)(2,1)} async-done(((bf16[256,256]{0,1:T(8,128)(2,1)}), bf16[2048,256]{0,1:T(8,128)(2,1)}) %all-gather.8.cloned.1.call-update) | async-done | bytes 1048592 | tf_op jit(solution)/shard_map/all_gather | solution.py:141
  103.2 26.7 %while.22 = (s32[]{:T(128)}, f32[2,5,256]{2,1,0:T(8,128)S(1)}, f32[2,5,256]{2,1,0:T(8,128)S(1)}, f32[2,5,256,128]{3,2,1,0:T(8,128)}, s32[]{:T(128)}, /*index=5*/...) while((s32[]{:T(128)}, f32[2,5,256]{2,1,0:T(8,128)S(1)}, ...), condition=%wide.region_14.15_spmd.clone, body=%wide.region_7.14_spmd.clone.sunk | while | flops 689325376 | bytes 31768368 | solution.py:157
  105.6 7.3 %conditional.3 = ((f32[2,5,256]{2,1,0:T(8,128)S(1)}, f32[2,5,256]{2,1,0:T(8,128)S(1)}, f32[2,5,256,128]{3,2,1,0:T(8,128)})) conditional(s32[]{:T(128)} %convert_element_type.104, (f32[2,5,256]{2,1,0:T(8,128)S(1)}, f32[2,5,256]{2,1,0:T(8,128)S(1)}, f32[2,5,256,128]{3,2,1,0:T(8,128)}) %tuple.92, (s32[]{:T(128)}, s32[8]{0:T(128)S(1)}, ...), branch_computations={%region_8.8_spmd, %region_9.13_spmd} | conditional | flops 689325376 | bytes 31767018 | solution.py:150
  109.6 2.2 %fusion.8 = f32[2,5,256,128]{3,2,1,0:T(8,128)S(1)} fusion(bf16[512,2,128,1]{0,2,3,1:T(8,128)(2,1)S(1)} %bitcast.69, f32[2,512,256,5]{2,1,3,0:T(8,128)S(1)} %get-tuple-element.678, f32[2,5,256]{2,1,0:T(8,128)S(1)} %max.5, pred[256,512]{0,1:T(8,128)(4,1)S(1)} %and_and_fusion, f32[2,5,256,128]{3,2,1,0:T(8,128)S(1)} %copy-done.1, ...), kind=kOutput, calls=%fused_computation.8 | convolution fusion | flops 342753280 | bytes 8278016 | tf_op jit(solution)/shard_map/while/body/eval_jaxpr/cond/branch_1_fun/cgqt,tch->cgqh/dot_general | solution.py:123
  114.1 7.3 %conditional.3 = ((f32[2,5,256]{2,1,0:T(8,128)S(1)}, f32[2,5,256]{2,1,0:T(8,128)S(1)}, f32[2,5,256,128]{3,2,1,0:T(8,128)})) conditional(s32[]{:T(128)} %convert_element_type.104, (f32[2,5,256]{2,1,0:T(8,128)S(1)}, f32[2,5,256]{2,1,0:T(8,128)S(1)}, f32[2,5,256,128]{3,2,1,0:T(8,128)}) %tuple.92, (s32[]{:T(128)}, s32[8]{0:T(128)S(1)}, ...), branch_computations={%region_8.8_spmd, %region_9.13_spmd} | conditional | flops 689325376 | bytes 31767018 | solution.py:150
  118.1 2.2 %fusion.8 = f32[2,5,256,128]{3,2,1,0:T(8,128)S(1)} fusion(bf16[512,2,128,1]{0,2,3,1:T(8,128)(2,1)S(1)} %bitcast.69, f32[2,512,256,5]{2,1,3,0:T(8,128)S(1)} %get-tuple-element.678, f32[2,5,256]{2,1,0:T(8,128)S(1)} %max.5, pred[256,512]{0,1:T(8,128)(4,1)S(1)} %and_and_fusion, f32[2,5,256,128]{3,2,1,0:T(8,128)S(1)} %copy-done.1, ...), kind=kOutput, calls=%fused_computation.8 | convolution fusion | flops 342753280 | bytes 8278016 | tf_op jit(solution)/shard_map/while/body/eval_jaxpr/cond/branch_1_fun/cgqt,tch->cgqh/dot_general | solution.py:123
  122.6 7.3 %conditional.3 = ((f32[2,5,256]{2,1,0:T(8,128)S(1)}, f32[2,5,256]{2,1,0:T(8,128)S(1)}, f32[2,5,256,128]{3,2,1,0:T(8,128)})) conditional(s32[]{:T(128)} %convert_element_type.104, (f32[2,5,256]{2,1,0:T(8,128)S(1)}, f32[2,5,256]{2,1,0:T(8,128)S(1)}, f32[2,5,256,128]{3,2,1,0:T(8,128)}) %tuple.92, (s32[]{:T(128)}, s32[8]{0:T(128)S(1)}, ...), branch_computations={%region_8.8_spmd, %region_9.13_spmd} | conditional | flops 689325376 | bytes 31767018 | solution.py:150
  126.6 2.2 %fusion.8 = f32[2,5,256,128]{3,2,1,0:T(8,128)S(1)} fusion(bf16[512,2,128,1]{0,2,3,1:T(8,128)(2,1)S(1)} %bitcast.69, f32[2,512,256,5]{2,1,3,0:T(8,128)S(1)} %get-tuple-element.678, f32[2,5,256]{2,1,0:T(8,128)S(1)} %max.5, pred[256,512]{0,1:T(8,128)(4,1)S(1)} %and_and_fusion, f32[2,5,256,128]{3,2,1,0:T(8,128)S(1)} %copy-done.1, ...), kind=kOutput, calls=%fused_computation.8 | convolution fusion | flops 342753280 | bytes 8278016 | tf_op jit(solution)/shard_map/while/body/eval_jaxpr/cond/branch_1_fun/cgqt,tch->cgqh/dot_general | solution.py:123
  129.9 2.8 %copy.40 = f32[2,5,256,128]{2,3,1,0:T(8,128)} copy(f32[2,5,256,128]{3,2,1,0:T(8,128)} %get-tuple-element.563) | data formatting | bytes 2621440 | tf_op jit(solution)/shard_map/while | solution.py:157
  132.7 1.4 broadcast_divide_fusion
  135.4 2.3 %copy.43 = bf16[2048,256]{1,0:T(8,128)(2,1)} copy(bf16[2048,256]{0,1:T(8,128)(2,1)} %get-tuple-element.837) | data formatting | bytes 2097152 | tf_op jit(solution)/shard_map/all_gather | solution.py:141
  137.7 2.3 %reshape.211 = bf16[16,32768]{1,0:T(8,128)(2,1)} reshape(bf16[2048,256]{1,0:T(8,128)(2,1)} %copy.43) | data formatting | bytes 2097152 | tf_op jit(solution)/shard_map/reshape | solution.py:168
  140.0 2.3 %copy.41 = bf16[2048,256]{1,0:T(8,128)(2,1)} copy(bf16[2048,256]{0,1:T(8,128)(2,1)} %get-tuple-element.835) | data formatting | bytes 2097152 | tf_op jit(solution)/shard_map/all_gather | solution.py:140
  142.3 2.3 %reshape.209 = bf16[16,32768]{1,0:T(8,128)(2,1)} reshape(bf16[2048,256]{1,0:T(8,128)(2,1)} %copy.41) | data formatting | bytes 2097152 | tf_op jit(solution)/shard_map/reshape | solution.py:165
  144.7 1.6 %fusion.23 = bf16[2,1,128,256]{3,0,2,1:T(2,128)(2,1)S(1)} fusion(bf16[2,128,8,256]{3,2,1,0:T(8,128)(2,1)} %bitcast.71, s32[16]{0:T(128)S(1)} %copy-done.4, s32[2]{0:T(128)S(1)} %iota_add_fusion.2), kind=kOutput, calls=%fused_computation.37 | convolution fusion | flops 2162720 | bytes 1179720 | tf_op jit(solution)/shard_map/dot_general | solution.py:167
  146.3 1.6 %fusion.22 = bf16[2,1,128,256]{3,0,2,1:T(2,128)(2,1)S(1)} fusion(bf16[2,128,8,256]{3,2,1,0:T(8,128)(2,1)} %bitcast.72, s32[16]{0:T(128)S(1)} %copy-done.4, s32[2]{0:T(128)S(1)} %iota_add_fusion.2), kind=kOutput, calls=%fused_computation.36 | convolution fusion | flops 2162720 | bytes 1179720 | tf_op jit(solution)/shard_map/dot_general | solution.py:164
  (93 shorter events, 27.4 us)
Async XLA Ops:
  7.2 43.9 %copy-start = (bf16[5120,256]{1,0:T(8,128)(2,1)S(1)}, bf16[5120,256]{1,0:T(8,128)(2,1)}, u32[]{:S(2)}) copy-start(bf16[5120,256]{1,0:T(8,128)(2,1)} %param.17) | copy-start | bytes 7864324
  7.2 43.9 %all-gather.4.cloned.1.call-start = ((), (), s32[]{:S(2)}) async-start(), calls=%async_computation | async-start | bytes 3276800 | tf_op jit(solution)/shard_map/all_gather | solution.py:68
  10.2 67.6 %all-gather.6.cloned.1.call-start = ((), (), s32[]{:S(2)}) async-start(), calls=%async_computation.1 | async-start | bytes 1179648 | tf_op jit(solution)/shard_map/all_gather | solution.py:140
  23.4 31.5 %copy-start.6 = (bf16[256]{0:T(256)(128)(2,1)S(1)}, bf16[256]{0:T(256)(128)(2,1)}, u32[]{:S(2)}) copy-start(bf16[256]{0:T(256)(128)(2,1)} %param.21) | copy-start | bytes 1540
  54.8 47.2 %all-gather.8.cloned.1.call-start = ((), (), s32[]{:S(2)}) async-start(), calls=%async_computation.2 | async-start | bytes 1179648 | tf_op jit(solution)/shard_map/all_gather | solution.py:141
  54.9 5.0 %copy-start.3 = (bf16[1280]{0:T(1024)(128)(2,1)S(1)}, bf16[1280]{0:T(1024)(128)(2,1)}, u32[]{:S(2)}) copy-start(bf16[1280]{0:T(1024)(128)(2,1)} %param.19) | copy-start | bytes 7684
  73.0 30.2 %copy-start.5 = (s32[8]{0:T(128)S(1)}, s32[8]{0:T(128)}, u32[]{:S(2)}) copy-start(s32[8]{0:T(128)} %param.22) | copy-start | bytes 100
  108.3 1.3 copy-start.1
  111.8 1.1 copy-start.2
  116.8 1.3 copy-start.1
  120.3 1.1 copy-start.2
  125.3 1.3 copy-start.1
  128.8 1.1 copy-start.2
  140.0 4.6 %copy-start.4 = (s32[16]{0:T(128)S(1)}, s32[16]{0:T(128)}, u32[]{:S(2)}) copy-start(s32[16]{0:T(128)} %param.23) | copy-start | bytes 196
Sparse Core Ops, SparseCore 0:
  10.4 40.6 all-gather.3
  54.9 22.8 all-gather.5
  79.4 22.5 all-gather.7
where the time goes:
time: 154 us; the launch traced here: 155 us
  waiting for transfers between devices  53 us (34%)
  matrix products  30.6 us (20%)
  local copies, waits for them, and re-layouts  25.7 us (17%)
  other arithmetic  17.1 us (11%)
  between operations  13.9 us (9%)
  blocking collectives  9.88 us (6%)
  loops' own time  5.11 us (3%)
    all_gather x1, waiting for transfers between devices, on_device(): piece = lax.all_gather(scaled, 'tp', axis=1, tiled=True)  27.7 us
    all_gather x1, waiting for transfers between devices, on_device(): value_piece = lax.all_gather(value, 'blk', axis=0, tiled=True)  24.2 us
    dot_general x3, matrix products, on_device(): totals.append(jnp.dot(piece, weight, preferred_element_type=jnp.float32))  17.6 us
    psum x1, blocking collectives, on_device(): squares = lax.psum(jnp.sum(wide * wide, axis=1), 'tp')  9.88 us
    dot_general x3, matrix products, attend(): jnp.einsum('cgqt,tch->cgqh', expo.astype(jnp.bfloat16), value_block.resha...  6.67 us
    another operation x1, loops' own time, on_device(): lax.fori_loop(0, count // step, one_step, (start_state[0], start_state[1]...  4.77 us
    reduce_sum x3, other arithmetic, attend(): total = total * shrink + jnp.sum(expo, axis=3)  3.77 us
    unnamed x13, local copies, waits for them, and re-layouts  3.24 us
  transfers between devices with their start and end apart: 3, of which 3 were waited for; matrix products, arithmetic and copies ran while one was open for 16% of the time, Pallas kernels for 0%

commit v1 on v0

--- a/solution.py
+++ b/solution.py
@@ -1,7 +1,7 @@
 import jax
 import jax.numpy as jnp
 from jax import lax
-from jax.sharding import PartitionSpec as P
+from jax.sharding import Mesh, PartitionSpec as P
 
 D = 5120
 HEADS = 40
@@ -49,8 +49,10 @@
     page_table,
 ):
     rows = tokens.shape[0]
-    blocks = lax.axis_size("blk")
-    me = lax.axis_index("blk")
+    chips = lax.axis_size("chip")
+    cores = lax.axis_size("core")
+    blocks = chips * cores
+    me = lax.axis_index("chip") * cores + lax.axis_index("core")
     q_width = w_query.shape[1]
     kv_width = w_key.shape[1]
     kv_dev = kv_width // HEAD
@@ -60,18 +62,32 @@
     scale = 1.0 / float(HEAD) ** 0.5
     wide = tokens.astype(jnp.float32)
     scaled = (wide * norm_gain.astype(jnp.float32)).astype(jnp.bfloat16)
-    empty = (
-        jnp.zeros((rows, q_width), jnp.float32),
-        jnp.zeros((rows, kv_width), jnp.float32),
-        jnp.zeros((rows, kv_width), jnp.float32),
-    )
-    piece = lax.all_gather(scaled, "tp", axis=1, tiled=True)
-    count = piece.shape[1]
-    totals = []
-    for total, weight in zip(empty, (w_query, w_key, w_value)):
-        totals.append(jnp.dot(piece, weight, preferred_element_type=jnp.float32))
+    part_sq = jnp.sum(wide * wide, axis=1)
+    width = tokens.shape[1]
+    parts = lax.axis_size("tp")
+    mine = lax.axis_index("tp")
+    weights = (w_query, w_key, w_value)
+
+    def project(chunk, source):
+        return [
+            jnp.dot(
+                chunk,
+                lax.dynamic_slice_in_dim(weight, source * width, width, 0),
+                preferred_element_type=jnp.float32,
+            )
+            for weight in weights
+        ]
+
+    totals = project(scaled, mine)
+    squares = part_sq
+    for shift in range(1, parts):
+        perm = [(j, (j + shift) % parts) for j in range(parts)]
+        got = lax.ppermute(scaled, "tp", perm)
+        got_sq = lax.ppermute(part_sq, "tp", perm)
+        more = project(got, (mine + parts - shift) % parts)
+        totals = [a + b for a, b in zip(totals, more)]
+        squares = squares + got_sq
     proj_query, proj_key, proj_value = tuple(totals)
-    squares = lax.psum(jnp.sum(wide * wide, axis=1), "tp")
     rstd = lax.rsqrt(squares / D + norm_eps)
     own_pos = me * rows + jnp.arange(rows, dtype=jnp.int32)
     own_seg, own_off = token_meta(own_pos, lengths)
@@ -137,8 +153,12 @@
         jnp.zeros((slots, PAGE * kv_width), jnp.float32),
         jnp.zeros((slots, PAGE * kv_width), jnp.float32),
     )
-    key_piece = lax.all_gather(key, "blk", axis=0, tiled=True)
-    value_piece = lax.all_gather(value, "blk", axis=0, tiled=True)
+    both = jnp.concatenate([key, value], axis=1)
+    both = lax.all_gather(both, "chip", axis=0, tiled=False)
+    both = lax.all_gather(both, "core", axis=1, tiled=False)
+    both = both.reshape(blocks * rows, 2 * kv_width)
+    key_piece = both[:, :kv_width]
+    value_piece = both[:, kv_width:]
     count = key_piece.shape[0]
     step = 512
 
@@ -180,8 +200,13 @@
 
 
 def solution(mesh):
+    blocks = mesh.shape["blk"]
+    split = Mesh(
+        mesh.devices.reshape(blocks // 2, 2, mesh.shape["tp"]), ("chip", "core", "tp")
+    )
+    blk = ("chip", "core")
     in_specs = (
-        P("blk", "tp"),
+        P(blk, "tp"),
         P("tp"),
         P(None, "tp"),
         P(None, "tp"),
@@ -192,7 +217,7 @@
         P(),
         P(),
     )
-    out_specs = (P("blk", "tp"), P("blk", None, None, "tp"))
+    out_specs = (P(blk, "tp"), P(blk, None, None, "tp"))
     return jax.shard_map(
-        on_device, mesh=mesh, in_specs=in_specs, out_specs=out_specs, check_vma=False
-    )
+        on_device, mesh=split, in_specs=in_specs, out_specs=out_specs, check_vma=False
+    )

time: 154 us -> 170 us (1.10)
  the two profiles are of different devices: /device:TPU:24 before, /device:TPU:8 now
where the time goes in v1:
time: 170 us; the launch traced here: 167 us
  waiting for transfers between devices  57.6 us (34%)
  matrix products  33.2 us (20%)
  local copies, waits for them, and re-layouts  30 us (18%)
  other arithmetic  19.1 us (11%)
  between operations  14.4 us (8%)
  starting transfers between devices  7.65 us (4%)
  loops' own time  5.23 us (3%)
    all_gather x1, waiting for transfers between devices, on_device(): both = lax.all_gather(both, 'chip', axis=0, tiled=False)  32.9 us
    dot_general x12, matrix products, project(): jnp.dot(chunk, lax.dynamic_slice_in_dim(weight, source * width, width, 0)...  23.5 us
    ppermute x3, waiting for transfers between devices, on_device(): got_sq = lax.ppermute(part_sq, 'tp', perm)  14.1 us
    ppermute x3, waiting for transfers between devices, on_device(): got = lax.ppermute(scaled, 'tp', perm)  10.6 us
    unnamed x38, local copies, waits for them, and re-layouts  5.5 us
    another operation x1, loops' own time, on_device(): lax.fori_loop(0, count // step, one_step, (start_state[0], start_state[1]...  4.98 us
    dot_general x2, matrix products, attend(): jnp.einsum('cgqt,tch->cgqh', expo.astype(jnp.bfloat16), value_block.resha...  4.45 us
    ppermute x3, starting transfers between devices, on_device(): got = lax.ppermute(scaled, 'tp', perm)  3.9 us
  transfers between devices with their start and end apart: 8, of which 3 were waited for; matrix products, arithmetic and copies ran while one was open for 21% of the time, Pallas kernels for 0%

profile of v1, /device:TPU:8, one launch (start us, length us, event | category | flops | bytes accessed | tf_op | source)
XLA Modules:
  0.0 167.3 jit_solution(12617613938328766203)
XLA Ops:
  8.1 2.1 %fusion.31 = (f32[256]{0:T(256)S(1)}, bf16[256,1280]{1,0:T(8,128)(2,1)}) fusion(bf16[256,1280]{1,0:T(8,128)(2,1)} %param.14, f32[1280]{0:T(1024)S(1)} %convert_element_type.73), kind=kLoop, calls=%fused_computation.33 | loop fusion | flops 1638144 | bytes 1316864 | tf_op jit(solution)/shard_map/reduce_sum | solution.py:65
  10.2 2.4 %collective-permute-start.5 = (bf16[256,1280]{1,0:T(8,128)(2,1)}, bf16[256,1280]{1,0:T(8,128)(2,1)}, u32[]{:S(2)}, u32[]{:S(2)}) collective-permute-start(bf16[256,1280]{1,0:T(8,128)(2,1)} %get-tuple-element.688), channel_id=1, source_target_pairs={{0,3},{1,0},{2,1},{3,2},{4,7},{5,4},{6,5},{7,6},{8,11},{9,8},{10,9... | collective-permute-start | bytes 1966088 | tf_op jit(solution)/shard_map/ppermute | solution.py:85
  12.6 2.9 %collective-permute-start.2 = (f32[256]{0:T(256)S(1)}, f32[256]{0:T(256)S(1)}, u32[]{:S(2)}, u32[]{:S(2)}) collective-permute-start(f32[256]{0:T(256)S(1)} %get-tuple-element.687), channel_id=1, source_target_pairs={{0,3},{1,0},{2,1},{3,2},{4,7},{5,4},{6,5},{7,6},{8,11},{9,8},{10,9... | collective-permute-start | bytes 3080 | tf_op jit(solution)/shard_map/ppermute | solution.py:86
  20.4 2.2 %fusion.58 = f32[256,256]{0,1:T(8,128)} fusion(bf16[256,1280]{1,0:T(8,128)(2,1)} %get-tuple-element.688, bf16[5120,256]{1,0:T(8,128)(2,1)S(1)} %copy-done, s32[]{:T(128)S(6)} %select_n.83), kind=kOutput, calls=%fused_computation.72 | convolution fusion | flops 167772160 | bytes 1572868 | tf_op jit(solution)/shard_map/dot_general | solution.py:73
  26.9 14.1 %collective-permute-done.2 = f32[256]{0:T(256)S(1)} collective-permute-done((f32[256]{0:T(256)S(1)}, f32[256]{0:T(256)S(1)}, u32[]{:S(2)}, u32[]{:S(2)}) %collective-permute-start.2) | collective-permute-done | bytes 1056 | tf_op jit(solution)/shard_map/ppermute | solution.py:86
  46.2 10.6 %collective-permute-done.4 = bf16[256,1280]{1,0:T(8,128)(2,1)S(1)} collective-permute-done((bf16[256,1280]{1,0:T(8,128)(2,1)}, bf16[256,1280]{1,0:T(8,128)(2,1)S(1)}, u32[]{:S(2)}, u32[]{:S(2)}) %collective-permute-start.4) | collective-permute-done | bytes 655392 | tf_op jit(solution)/shard_map/ppermute | solution.py:85
  60.7 32.9 %all-gather.5.cloned.1.call-done = bf16[1024,512]{0,1:T(8,128)(2,1)} async-done(((bf16[256,512]{0,1:T(8,128)(2,1)}), bf16[1024,512]{0,1:T(8,128)(2,1)}) %all-gather.5.cloned.1.call-update) | async-done | bytes 1048592 | tf_op jit(solution)/shard_map/all_gather | solution.py:157
  93.6 2.7 %reshape.217 = bf16[4,256,512]{1,0,2:T(4,128)(2,1)} reshape(bf16[1024,512]{0,1:T(8,128)(2,1)} %all-gather.5.cloned.1.call-done) | data formatting | bytes 2097152 | tf_op jit(solution)/shard_map/all_gather | solution.py:157
  96.3 3.2 %fusion.20 = f32[256,1280]{1,0:T(8,128)S(1)} fusion(bf16[256,1280]{1,0:T(8,128)(2,1)} %get-tuple-element.688, bf16[5120,1280]{1,0:T(8,128)(2,1)} %param.16, s32[]{:T(128)S(6)} %select_n.83), kind=kOutput, calls=%fused_computation.26 | convolution fusion | flops 838860800 | bytes 5242884 | tf_op jit(solution)/shard_map/dot_general | solution.py:73
  99.5 3.6 %fusion.14 = f32[256,1280]{1,0:T(8,128)S(1)} fusion(bf16[256,1280]{1,0:T(8,128)(2,1)} %collective-permute-done.5, bf16[5120,1280]{1,0:T(8,128)(2,1)} %param.16, s32[]{:T(128)S(6)} %select_n.89), kind=kOutput, calls=%fused_computation.20 | convolution fusion | flops 838860800 | bytes 5242884 | tf_op jit(solution)/shard_map/dot_general | solution.py:73
  103.1 2.9 %fusion.16 = f32[256,1280]{1,0:T(8,128)S(1)} fusion(bf16[256,1280]{1,0:T(8,128)(2,1)S(1)} %copy-done.5, bf16[5120,1280]{1,0:T(8,128)(2,1)} %param.16, s32[]{:T(128)S(6)} %select_n.87), kind=kOutput, calls=%fused_computation.22 | convolution fusion | flops 838860800 | bytes 5242884 | tf_op jit(solution)/shard_map/dot_general | solution.py:73
  106.1 4.1 %multiply_add_fusion.1 = f32[256,1280]{1,0:T(8,128)} fusion(f32[1280]{0:T(1024)S(1)} %convert_element_type.80, f32[256]{0:T(256)S(1)} %add_rsqrt_fusion, f32[256,1280]{1,0:T(8,128)S(1)} %fusion.14, f32[256,1280]{1,0:T(8,128)S(1)} %fusion.16, f32[256,1280]{1,0:T(8,128)S(1)} %fusion.20, bf16[256,1280]{1,0:T(8,128)(2,1)S(1)} %collective-permute-done.3, ...), kind=kOutput, calls=%fused_computation.37 | convolution fusion | flops 840499200 | bytes 9181188 | tf_op jit(solution)/shard_map/dot_general | solution.py:73
  110.2 2.8 %copy.44 = f32[256,1280]{0,1:T(8,128)} copy(f32[256,1280]{1,0:T(8,128)} %multiply_add_fusion.1) | data formatting | bytes 2621440 | tf_op jit(solution)/shard_map/add | solution.py:95
  116.8 2.2 %copy.62 = bf16[64,8,4,512]{3,1,2,0:T(8,128)(2,1)S(1)} copy(bf16[64,8,4,512]{3,2,1,0:T(4,128)(2,1)} %bitcast.87) | data formatting | bytes 4194304
  120.5 2.3 %copy.49 = bf16[2048,256]{1,0:T(8,128)(2,1)} copy(bf16[2048,256]{0,1:T(8,128)(2,1)} %get-tuple-element.798) | data formatting | bytes 2097152 | tf_op jit(solution)/shard_map/slice | solution.py:161
  122.8 2.3 %copy.47 = bf16[2048,256]{1,0:T(8,128)(2,1)} copy(bf16[2048,256]{0,1:T(8,128)(2,1)} %get-tuple-element.796) | data formatting | bytes 2097152 | tf_op jit(solution)/shard_map/slice | solution.py:160
  126.3 19.6 %while.22 = (s32[]{:T(128)}, f32[2,5,256]{2,1,0:T(8,128)S(1)}, f32[2,5,256]{2,1,0:T(8,128)S(1)}, f32[2,5,256,128]{3,2,1,0:T(8,128)}, s32[]{:T(128)}, /*index=5*/...) while((s32[]{:T(128)}, f32[2,5,256]{2,1,0:T(8,128)S(1)}, ...), condition=%wide.region_13.14_spmd.clone, body=%wide.region_6.13_spmd.clone.sunk | while | flops 689325376 | bytes 31768368 | solution.py:177
  127.5 7.3 %conditional.3 = ((f32[2,5,256]{2,1,0:T(8,128)S(1)}, f32[2,5,256]{2,1,0:T(8,128)S(1)}, f32[2,5,256,128]{3,2,1,0:T(8,128)})) conditional(s32[]{:T(128)} %convert_element_type.104, (f32[2,5,256]{2,1,0:T(8,128)S(1)}, f32[2,5,256]{2,1,0:T(8,128)S(1)}, f32[2,5,256,128]{3,2,1,0:T(8,128)}) %tuple.95, (s32[]{:T(128)}, s32[8]{0:T(128)S(1)}, ...), branch_computations={%region_7.7_spmd, %region_8.12_spmd} | conditional | flops 689325376 | bytes 31767018 | solution.py:170
  131.5 2.2 %fusion.8 = f32[2,5,256,128]{3,2,1,0:T(8,128)S(1)} fusion(bf16[512,2,128,1]{0,2,3,1:T(8,128)(2,1)S(1)} %bitcast.82, f32[2,512,256,5]{2,1,3,0:T(8,128)S(1)} %get-tuple-element.680, f32[2,5,256]{2,1,0:T(8,128)S(1)} %max.5, pred[256,512]{0,1:T(8,128)(4,1)S(1)} %and_and_fusion, f32[2,5,256,128]{3,2,1,0:T(8,128)S(1)} %copy-done.1, ...), kind=kOutput, calls=%fused_computation.8 | convolution fusion | flops 342753280 | bytes 8278016 | tf_op jit(solution)/shard_map/while/body/eval_jaxpr/cond/branch_1_fun/cgqt,tch->cgqh/dot_general | solution.py:139
  136.1 7.3 %conditional.3 = ((f32[2,5,256]{2,1,0:T(8,128)S(1)}, f32[2,5,256]{2,1,0:T(8,128)S(1)}, f32[2,5,256,128]{3,2,1,0:T(8,128)})) conditional(s32[]{:T(128)} %convert_element_type.104, (f32[2,5,256]{2,1,0:T(8,128)S(1)}, f32[2,5,256]{2,1,0:T(8,128)S(1)}, f32[2,5,256,128]{3,2,1,0:T(8,128)}) %tuple.95, (s32[]{:T(128)}, s32[8]{0:T(128)S(1)}, ...), branch_computations={%region_7.7_spmd, %region_8.12_spmd} | conditional | flops 689325376 | bytes 31767018 | solution.py:170
  140.1 2.2 %fusion.8 = f32[2,5,256,128]{3,2,1,0:T(8,128)S(1)} fusion(bf16[512,2,128,1]{0,2,3,1:T(8,128)(2,1)S(1)} %bitcast.82, f32[2,512,256,5]{2,1,3,0:T(8,128)S(1)} %get-tuple-element.680, f32[2,5,256]{2,1,0:T(8,128)S(1)} %max.5, pred[256,512]{0,1:T(8,128)(4,1)S(1)} %and_and_fusion, f32[2,5,256,128]{3,2,1,0:T(8,128)S(1)} %copy-done.1, ...), kind=kOutput, calls=%fused_computation.8 | convolution fusion | flops 342753280 | bytes 8278016 | tf_op jit(solution)/shard_map/while/body/eval_jaxpr/cond/branch_1_fun/cgqt,tch->cgqh/dot_general | solution.py:139
  145.9 2.8 %copy.46 = f32[2,5,256,128]{2,3,1,0:T(8,128)} copy(f32[2,5,256,128]{3,2,1,0:T(8,128)} %get-tuple-element.563) | data formatting | bytes 2621440 | tf_op jit(solution)/shard_map/while | solution.py:177
  151.4 2.3 %reshape.215 = bf16[16,32768]{1,0:T(8,128)(2,1)} reshape(bf16[2048,256]{1,0:T(8,128)(2,1)} %copy.49) | data formatting | bytes 2097152 | tf_op jit(solution)/shard_map/reshape | solution.py:188
  153.8 2.4 %reshape.213 = bf16[16,32768]{1,0:T(8,128)(2,1)} reshape(bf16[2048,256]{1,0:T(8,128)(2,1)} %copy.47) | data formatting | bytes 2097152 | tf_op jit(solution)/shard_map/reshape | solution.py:185
  (121 shorter events, 42.4 us)
Async XLA Ops:
  7.2 13.3 %copy-start = (bf16[5120,256]{1,0:T(8,128)(2,1)S(1)}, bf16[5120,256]{1,0:T(8,128)(2,1)}, u32[]{:S(2)}) copy-start(bf16[5120,256]{1,0:T(8,128)(2,1)} %param.17) | copy-start | bytes 7864324
  7.2 86.4 %all-gather.5.cloned.1.call-start = ((), (), s32[]{:S(2)}) async-start(), calls=%async_computation | async-start | bytes 1310720 | tf_op jit(solution)/shard_map/all_gather | solution.py:157
  10.2 33.0 %collective-permute-start.5 = (bf16[256,1280]{1,0:T(8,128)(2,1)}, bf16[256,1280]{1,0:T(8,128)(2,1)}, u32[]{:S(2)}, u32[]{:S(2)}) collective-permute-start(bf16[256,1280]{1,0:T(8,128)(2,1)} %get-tuple-element.688), channel_id=1, source_target_pairs={{0,3},{1,0},{2,1},{3,2},{4,7},{5,4},{6,5},{7,6},{8,11},{9,8},{10,9... | collective-permute-start | bytes 1966088 | tf_op jit(solution)/shard_map/ppermute | solution.py:85
  12.6 32.1 %collective-permute-start.3 = (bf16[256,1280]{1,0:T(8,128)(2,1)}, bf16[256,1280]{1,0:T(8,128)(2,1)S(1)}, u32[]{:S(2)}, u32[]{:S(2)}) collective-permute-start(bf16[256,1280]{1,0:T(8,128)(2,1)} %get-tuple-element.688), channel_id=1, source_target_pairs={{0,1},{1,2},{2,3},{3,0},{4,5},{5,6},{6,7},{7,4},{8,9},{9,10},{10,1... | collective-permute-start | bytes 1966088 | tf_op jit(solution)/shard_map/ppermute | solution.py:85
  12.6 28.4 %collective-permute-start.2 = (f32[256]{0:T(256)S(1)}, f32[256]{0:T(256)S(1)}, u32[]{:S(2)}, u32[]{:S(2)}) collective-permute-start(f32[256]{0:T(256)S(1)} %get-tuple-element.687), channel_id=1, source_target_pairs={{0,3},{1,0},{2,1},{3,2},{4,7},{5,4},{6,5},{7,6},{8,11},{9,8},{10,9... | collective-permute-start | bytes 3080 | tf_op jit(solution)/shard_map/ppermute | solution.py:86
  15.6 26.9 %collective-permute-start.1 = (f32[256]{0:T(256)S(1)}, f32[256]{0:T(256)}, u32[]{:S(2)}, u32[]{:S(2)}) collective-permute-start(f32[256]{0:T(256)S(1)} %get-tuple-element.687), channel_id=1, source_target_pairs={{0,2},{1,3},{2,0},{3,1},{4,6},{5,7},{6,4},{7,5},{8,10},{9,11},{10,... | collective-permute-start | bytes 3080 | tf_op jit(solution)/shard_map/ppermute | solution.py:86
  16.1 26.4 %collective-permute-start = (f32[256]{0:T(256)S(1)}, f32[256]{0:T(256)}, u32[]{:S(2)}, u32[]{:S(2)}) collective-permute-start(f32[256]{0:T(256)S(1)} %get-tuple-element.687), channel_id=1, source_target_pairs={{0,1},{1,2},{2,3},{3,0},{4,5},{5,6},{6,7},{7,4},{8,9},{9,10},{10,1... | collective-permute-start | bytes 3080 | tf_op jit(solution)/shard_map/ppermute | solution.py:86
  18.7 3.9 %copy-start.16 = (s32[8]{0:T(128)S(1)}, s32[8]{0:T(128)}, u32[]{:S(2)}) copy-start(s32[8]{0:T(128)} %param.22) | copy-start | bytes 100
  18.7 3.9 %copy-start.18 = (s32[8,1]{0,1:T(1,128)S(1)}, s32[8,1]{0,1:T(1,128)}, u32[]{:S(2)}) copy-start(s32[8,1]{0,1:T(1,128)} %reduce-window.18) | copy-start | bytes 100
  18.7 4.7 %copy-start.15 = (f32[64]{0:T(128)S(1)}, f32[64]{0:T(128)}, u32[]{:S(2)}) copy-start(f32[64]{0:T(128)} %multiply_power_fusion) | copy-start | bytes 772
  26.9 29.9 %copy-start.13 = (f32[256]{0:T(256)S(1)}, f32[256]{0:T(256)}, u32[]{:S(2)}) copy-start(f32[256]{0:T(256)} %convert_element_type.75) | copy-start | bytes 3076
  41.0 15.8 %collective-permute-start.4 = (bf16[256,1280]{1,0:T(8,128)(2,1)}, bf16[256,1280]{1,0:T(8,128)(2,1)S(1)}, u32[]{:S(2)}, u32[]{:S(2)}) collective-permute-start(bf16[256,1280]{1,0:T(8,128)(2,1)} %get-tuple-element.688), channel_id=1, source_target_pairs={{0,2},{1,3},{2,0},{3,1},{4,6},{5,7},{6,4},{7,5},{8,10},{9,11},{10,... | collective-permute-start | bytes 1966088 | tf_op jit(solution)/shard_map/ppermute | solution.py:85
  43.2 14.1 %copy-start.6 = (f32[256,64]{0,1:T(8,128)S(1)}, f32[256,64]{0,1:T(8,128)}, u32[]{:S(2)}) copy-start(f32[256,64]{0,1:T(8,128)} %get-tuple-element.691) | copy-start | bytes 196612
  43.2 14.1 %copy-start.8 = (f32[256,64]{0,1:T(8,128)S(1)}, f32[256,64]{0,1:T(8,128)}, u32[]{:S(2)}) copy-start(f32[256,64]{0,1:T(8,128)} %get-tuple-element.692) | copy-start | bytes 196612
  44.7 12.6 %copy-start.3 = (bf16[5120,256]{1,0:T(8,128)(2,1)S(1)}, bf16[5120,256]{1,0:T(8,128)(2,1)}, u32[]{:S(2)}) copy-start(bf16[5120,256]{1,0:T(8,128)(2,1)} %param.18) | copy-start | bytes 7864324
  56.8 2.5 %copy-start.4 = (bf16[256,1280]{1,0:T(8,128)(2,1)}, bf16[256,1280]{1,0:T(8,128)(2,1)S(1)}, u32[]{:S(2)}) copy-start(bf16[256,1280]{1,0:T(8,128)(2,1)S(1)} %collective-permute-done.4) | copy-start | bytes 1966084
  57.2 2.1 %copy-start.12 = (f32[256]{0:T(256)S(1)}, f32[256]{0:T(256)}, u32[]{:S(2)}) copy-start(f32[256]{0:T(256)} %convert_element_type.78) | copy-start | bytes 3076
  59.3 37.0 %copy-start.10 = (bf16[1280]{0:T(1024)(128)(2,1)S(1)}, bf16[1280]{0:T(1024)(128)(2,1)}, u32[]{:S(2)}) copy-start(bf16[1280]{0:T(1024)(128)(2,1)} %param.19) | copy-start | bytes 7684
  60.4 56.4 %all-gather.7.cloned.1.call-start = ((), (), s32[]{:S(2)}) async-start(), calls=%async_computation.1 | async-start | bytes 3145728 | tf_op jit(solution)/shard_map/all_gather | solution.py:158
  99.5 3.6 %copy-start.5 = (bf16[256,1280]{1,0:T(8,128)(2,1)S(1)}, bf16[256,1280]{1,0:T(8,128)(2,1)}, u32[]{:S(2)}) copy-start(bf16[256,1280]{1,0:T(8,128)(2,1)} %copy-done.4) | copy-start | bytes 1966084
  110.2 2.8 %copy-start.7 = (f32[256,64]{0,1:T(8,128)S(1)}, f32[256,64]{0,1:T(8,128)}, u32[]{:S(2)}) copy-start(f32[256,64]{0,1:T(8,128)} %get-tuple-element.691) | copy-start | bytes 196612
  110.2 2.8 %copy-start.9 = (f32[256,64]{0,1:T(8,128)S(1)}, f32[256,64]{0,1:T(8,128)}, u32[]{:S(2)}) copy-start(f32[256,64]{0,1:T(8,128)} %get-tuple-element.692) | copy-start | bytes 196612
  120.5 5.7 %copy-start.17 = (s32[8]{0:T(128)S(1)}, s32[8]{0:T(128)}, u32[]{:S(2)}) copy-start(s32[8]{0:T(128)} %param.22) | copy-start | bytes 100
  150.3 5.8 %copy-start.11 = (s32[16]{0:T(128)S(1)}, s32[16]{0:T(128)}, u32[]{:S(2)}) copy-start(s32[16]{0:T(128)} %param.23) | copy-start | bytes 196
  (5 other events, 6.2 us)
Sparse Core Ops, SparseCore 0:
  60.6 32.9 all-gather.4
  96.4 7.8 all-gather.6
